TPU v7x, 512 devices: a whole 4x8x8 slice. The times are simulated.
512 devices in a mesh: seq: 64 (over x, z_lo, y), tp: 8 (over z_hi, core).
Axes of the slice: x: 4, y: 8, z: 8 (z_hi: 4, z_lo: 2; z = z_hi * 2 + z_lo), core: 2. Of those that a mesh axis runs over, the one named last changes fastest.
Arguments:
- tokens: bfloat16 [16384, 2048], P('seq', 'tp'), may hold values from -6 to 6
- key_weight: bfloat16 [2048, 2048], P(None, 'tp'), may hold values from -0.125 to 0.125
- value_weight: bfloat16 [2048, 2048], P(None, 'tp'), may hold values from -0.125 to 0.125
- queries: bfloat16 [16384, 2, 2048], P('seq', None, 'tp'), may hold values from -256 to 256
- prompt_pages: int32 [16], replicated, may hold values from 1 to 97, 1024 in all
- page_table: int32 [1024], P('seq'), may hold values from 0 to 1023, as said below
Outputs:
- attended: bfloat16 [16384, 2, 2048], P('seq', None, 'tp')
- cache: bfloat16 [1024, 16, 2, 2048], P('seq', None, None, 'tp')
Inputs may be any that keep to these rules, and one draw needn't show every extreme that they name: `prompt_pages`: lengths of the prompts in pages; they sum to 1024 and the longest has exactly 97 pages. `page_table`: A permutation of the cache pages. Page c is held by owner c // 16 of seq. At most 1 pages of one stream block go to one owner, some block sends exactly 1 to one owner, and every owner receives 256/16 pages.
All inputs are finite; a program needn't handle non-finite values.
Results may differ from a plain program's by a relative error of at most 0.03.
Values may be sent and summed in bfloat16 or wider, within the bound.
No kernel may reach another device: no remote copies, remote signals or barrier semaphores. Data moves between devices by JAX's collectives and lax.ppermute only.
A program may use at most 64 MiB of HBM per device.

v0:
```python
import math
import jax
import jax.numpy as jnp
from jax import lax
from jax.sharding import PartitionSpec as P

HD = 128
TOPK = 2
PAGE = 16
BACK = 6


def from_behind(value, axis, by):
    peers = lax.axis_size(axis)
    pairs = [(i, i + by) for i in range(peers) if 0 <= i + by < peers]
    return lax.ppermute(value, axis, pairs)


def segment_info(positions, prompt_pages):
    ends = PAGE * jnp.cumsum(prompt_pages)
    below = ends[None, :] <= positions[:, None]
    segment = jnp.sum(below.astype(jnp.int32), axis=1)
    start = jnp.max(jnp.where(below, ends[None, :], 0), axis=1)
    return (segment, positions - start)


def rotate_heads(raw, offsets):
    half = HD // 2
    inverse = 10000.0 ** (-(2.0 * jnp.arange(half, dtype=jnp.float32)) / HD)
    angle = offsets.astype(jnp.float32)[:, None] * inverse[None, :]
    cosine = jnp.cos(angle)[:, None, :]
    sine = jnp.sin(angle)[:, None, :]
    lower = raw[..., :half]
    upper = raw[..., half:]
    return jnp.concatenate([lower * cosine - upper * sine, upper * cosine + lower * sine], axis=-1)


def body(tokens, key_weight, value_weight, queries, prompt_pages, page_table):
    block_rows = tokens.shape[0]
    width = key_weight.shape[1]
    local_heads = width // HD
    devices = lax.axis_size("seq")
    first_row = lax.axis_index("seq") * block_rows
    positions = first_row + jnp.arange(block_rows, dtype=jnp.int32)
    segment, offsets = segment_info(positions, prompt_pages)
    piece = lax.all_gather(tokens, "tp", axis=1, tiled=True)
    raw_keys = jnp.dot(piece, key_weight, preferred_element_type=jnp.float32)
    raw_values = jnp.dot(piece, value_weight, preferred_element_type=jnp.float32)
    keys = rotate_heads(raw_keys.reshape(block_rows, local_heads, HD), offsets).astype(jnp.bfloat16)
    values = raw_values.astype(jnp.bfloat16)
    key_value = jnp.stack([keys.reshape(block_rows, width), values], axis=1)
    blocks = [key_value]
    previous = key_value
    for distance in range(1, BACK + 1):
        previous = from_behind(previous, "seq", 1)
        blocks.append(previous)
    query = queries.reshape(block_rows, TOPK, local_heads, HD)
    scale = 1.0 / math.sqrt(HD)
    masks = []
    for distance in range(BACK + 1):
        key_place = positions - distance * block_rows
        key_segment, unused_offsets = segment_info(key_place, prompt_pages)
        allowed = (segment[:, None] == key_segment[None, :]) & (
            key_place[None, :] <= positions[:, None]
        )
        masks.append(allowed & (key_place[None, :] >= 0))

    def block_scores(expert_query, block, allowed):
        key_heads = block[:, 0].reshape(block_rows, local_heads, HD)
        scores = (
            jnp.einsum("qhd,khd->qhk", expert_query, key_heads, preferred_element_type=jnp.float32)
            * scale
        )
        return jnp.where(allowed[:, None, :], scores, -jnp.inf)

    outputs = []
    for expert in range(TOPK):
        expert_query = query[:, expert]
        score_list = []
        for distance in range(BACK + 1):
            block = blocks[distance]
            allowed = masks[distance]

            def compute(block=block, allowed=allowed):
                return block_scores(expert_query, block, allowed)

            score_list.append(compute())
        peak = jnp.max(score_list[0], axis=-1)
        for distance in range(1, BACK + 1):
            peak = jnp.maximum(peak, jnp.max(score_list[distance], axis=-1))
        total = jnp.zeros((block_rows, local_heads), jnp.float32)
        summed = jnp.zeros((block_rows, local_heads, HD), jnp.float32)
        for distance in range(BACK + 1):
            block = blocks[distance]
            allowed = masks[distance]
            scores = score_list[distance]

            def accumulate(state, block=block, scores=scores):
                weight = jnp.exp(scores - peak[..., None])
                rounded = weight.astype(jnp.bfloat16)
                value_heads = block[:, 1].reshape(block_rows, local_heads, HD)
                product = jnp.einsum(
                    "qhk,khd->qhd", rounded, value_heads, preferred_element_type=jnp.float32
                )
                return (state[0] + jnp.sum(weight, axis=-1), state[1] + product)

            total, summed = accumulate((total, summed))
        outputs.append((summed / total[..., None]).astype(jnp.bfloat16))
    attended = jnp.stack(outputs, axis=1).reshape(block_rows, TOPK, width)
    pages_dev = block_rows // PAGE
    capacity = max(1, pages_dev // devices)
    page_data = key_value.reshape(pages_dev, PAGE * 2 * width)
    owner = page_table // pages_dev
    place_on_owner = page_table % pages_dev
    page_order = jnp.arange(pages_dev, dtype=jnp.int32)
    earlier = (owner[:, None] == owner[None, :]) & (page_order[None, :] < page_order[:, None])
    rank = jnp.sum(earlier.astype(jnp.int32), axis=1)
    target = (owner[None, None, :] == jnp.arange(devices, dtype=jnp.int32)[:, None, None]) & (
        rank[None, None, :] == jnp.arange(capacity, dtype=jnp.int32)[None, :, None]
    )
    outgoing = jnp.einsum(
        "dcp,pf->dcf", target.astype(jnp.bfloat16), page_data, preferred_element_type=jnp.float32
    ).astype(jnp.bfloat16)
    labels = jnp.sum(jnp.where(target, place_on_owner[None, None, :] + 1, 0), axis=2) - 1
    incoming, arrived = (
        lax.all_to_all(outgoing, "seq", split_axis=0, concat_axis=0, tiled=True),
        lax.all_to_all(labels, "seq", split_axis=0, concat_axis=0, tiled=True),
    )
    placing = (arrived.reshape(-1)[None, :] == page_order[:, None]).astype(jnp.bfloat16)
    pool = jnp.dot(
        placing,
        incoming.reshape(devices * capacity, PAGE * 2 * width),
        preferred_element_type=jnp.float32,
    ).astype(jnp.bfloat16)
    cache = pool.reshape(pages_dev, PAGE, 2, width)
    return (attended, cache)


def solution(mesh):
    in_specs = (P("seq", "tp"), P(None, "tp"), P(None, "tp"), P("seq", None, "tp"), P(), P("seq"))
    out_specs = (P("seq", None, "tp"), P("seq", None, None, "tp"))
    return jax.shard_map(body, mesh=mesh, in_specs=in_specs, out_specs=out_specs, check_vma=False)
```

profile of v0, /device:TPU:6, one launch (start us, length us, event | category | flops | bytes accessed | tf_op | source)
XLA Modules:
  0.0 179.1 jit_solution(18239066020747687075)
XLA Ops:
  7.2 0.7 all-gather.2.cloned.1.call-update
  7.9 0.7 fusion.112
  8.9 0.7 copy.187
  9.6 12.6 %all-to-all-start = ((s32[64,1,1]{2,1,0:T(1,128)}), s32[64,1,1]{2,1,0:T(1,128)S(1)}, u32[]{:S(2)}, u32[]{:S(2)}) async-start(s32[64,1,1]{2,1,0:T(1,128)} %copy.187), calls=%async_computation | async-start | bytes 65536 | tf_op jit(solution)/shard_map/all_to_all | solution.py:127
  22.3 0.7 copy.152
  23.3 0.5 multiply_cosine_fusion
  23.9 2.1 %and_and_fusion.5 = (pred[256,256]{0,1:T(8,128)(4,1)}, pred[256,256]{0,1:T(8,128)(4,1)}, pred[256,256]{0,1:T(8,128)(4,1)}, pred[256,256]{0,1:T(8,128)(4,1)}, pre...) fusion(s32[256]{0:T(256)S(1)} %get-tuple-element.80, s32[256]{0:T(256)S(1)} %get-tuple-element.25, s32[256]{0:T(256)S(1)} %fusion.110, ...), kind=kLoop, calls=%fused_computation.134 | loop fusion | flops 1572864 | bytes 407040 | tf_op jit(solution)/shard_map/and | solution.py:66
  26.0 0.8 and_and_fusion.4
  26.7 1.1 copy.155
  27.9 2.7 %all-to-all-done = s32[64,1,1]{2,1,0:T(1,128)S(1)} async-done(((s32[64,1,1]{2,1,0:T(1,128)}), s32[64,1,1]{2,1,0:T(1,128)S(1)}, u32[]{:S(2)}, u32[]{:S(2)}) %all-to-all-start) | async-done | bytes 288 | tf_op jit(solution)/shard_map/all_to_all | solution.py:127
  30.6 1.8 %reduce.2 = s32[64]{0:T(128)} reduce(s32[64,1,1]{2,1,0:T(1,128)S(1)} %all-to-all-done, s32[]{:T(128)} %constant.64.clone.1), dimensions={1,2}, to_apply=%all_to_all.7.reduce_sub_computation | reduce | bytes 516 | tf_op jit(solution)/shard_map/all_to_all | solution.py:127
  32.4 16.9 %all-gather.2.cloned.1.call-done = bf16[256,2048]{1,0:T(8,128)(2,1)} async-done(((bf16[256,256]{1,0:T(8,128)(2,1)}), bf16[256,2048]{1,0:T(8,128)(2,1)}) %all-gather.2.cloned.1.call-update) | async-done | bytes 1048592 | tf_op jit(solution)/shard_map/all_gather | solution.py:46
  49.2 1.7 fusion.134
  51.5 0.6 copy-done.21
  52.3 1.7 convolution_convert_fusion.2
  54.0 0.7 pad_maximum_fusion
  54.7 3.4 %collective-permute-start = (bf16[256,2,256]{0,2,1:T(8,128)(2,1)}, bf16[256,2,256]{0,2,1:T(8,128)(2,1)}, u32[]{:S(2)}, u32[]{:S(2)}) collective-permute-start(bf16[256,2,256]{0,2,1:T(8,128)(2,1)} %pad_maximum_fusion), channel_id=1, source_target_pairs={{0,8},{8,16},{16,24},{24,32},{32,40},{40,48},{48,56},{56,64},{64,7... | collective-permute-start | bytes 786440 | tf_op jit(solution)/shard_map/ppermute | solution.py:16
  58.1 1.1 copy.188
  59.5 0.5 fusion
  60.0 0.6 broadcast.736
  60.6 1.4 reduce.4
  62.0 1.6 reshape.847
  63.6 9.9 %all-to-all-start.1 = ((bf16[64,2,4096]{2,1,0:T(2,128)(2,1)}), bf16[64,2,4096]{2,1,0:T(2,128)(2,1)}, u32[]{:S(2)}, u32[]{:S(2)}) async-start(bf16[64,2,4096]{2,1,0:T(2,128)(2,1)} %reshape.847), calls=%async_computation.1 | async-start | bytes 2097152 | tf_op jit(solution)/shard_map/all_to_all | solution.py:126
  73.8 1.6 fusion.125
  75.4 3.4 %collective-permute-start.1 = (bf16[256,2,256]{0,2,1:T(8,128)(2,1)}, bf16[256,2,256]{0,2,1:T(8,128)(2,1)S(1)}, u32[]{:S(2)}, u32[]{:S(2)}) collective-permute-start(bf16[256,2,256]{0,2,1:T(8,128)(2,1)} %collective-permute-done), channel_id=1, source_target_pairs={{0,8},{8,16},{16,24},{24,32},{32,40},{40,48},{48,56},{56,64},{64,7... | collective-permute-start | bytes 786440 | tf_op jit(solution)/shard_map/ppermute | solution.py:16
  78.7 1.0 fusion.118
  79.8 0.3 fusion.133
  80.0 0.3 fusion.126
  80.3 25.0 %collective-permute-done.1 = bf16[256,2,256]{0,2,1:T(8,128)(2,1)S(1)} collective-permute-done((bf16[256,2,256]{0,2,1:T(8,128)(2,1)}, bf16[256,2,256]{0,2,1:T(8,128)(2,1)S(1)}, u32[]{:S(2)}, u32[]{:S(2)}) %collective-permute-start.1) | collective-permute-done | bytes 262176 | tf_op jit(solution)/shard_map/ppermute | solution.py:16
  105.3 1.9 %collective-permute-start.2 = (bf16[256,2,256]{0,2,1:T(8,128)(2,1)S(1)}, bf16[256,2,256]{0,2,1:T(8,128)(2,1)S(1)}, u32[]{:S(2)}, u32[]{:S(2)}) collective-permute-start(bf16[256,2,256]{0,2,1:T(8,128)(2,1)S(1)} %collective-permute-done.1), channel_id=1, source_target_pairs={{0,8},{8,16},{16,24},{24,32},{32,40},{40,48},{48,56},{56,64},{64,7... | collective-permute-start | bytes 786440 | tf_op jit(solution)/shard_map/ppermute | solution.py:16
  107.3 0.3 fusion.131
  107.6 0.3 fusion.124
  107.9 9.7 %collective-permute-done.2 = bf16[256,2,256]{0,2,1:T(8,128)(2,1)S(1)} collective-permute-done((bf16[256,2,256]{0,2,1:T(8,128)(2,1)S(1)}, bf16[256,2,256]{0,2,1:T(8,128)(2,1)S(1)}, u32[]{:S(2)}, u32[]{:S(2)}) %collective-permute-start.2) | collective-permute-done | bytes 262176 | tf_op jit(solution)/shard_map/ppermute | solution.py:16
  117.6 1.9 %collective-permute-start.3 = (bf16[256,2,256]{0,2,1:T(8,128)(2,1)S(1)}, bf16[256,2,256]{0,2,1:T(8,128)(2,1)S(1)}, u32[]{:S(2)}, u32[]{:S(2)}) collective-permute-start(bf16[256,2,256]{0,2,1:T(8,128)(2,1)S(1)} %collective-permute-done.2), channel_id=1, source_target_pairs={{0,8},{8,16},{16,24},{24,32},{32,40},{40,48},{48,56},{56,64},{64,7... | collective-permute-start | bytes 786440 | tf_op jit(solution)/shard_map/ppermute | solution.py:16
  119.5 0.3 fusion.130
  119.8 0.3 fusion.123
  120.1 8.8 %collective-permute-done.3 = bf16[256,2,256]{0,2,1:T(8,128)(2,1)S(1)} collective-permute-done((bf16[256,2,256]{0,2,1:T(8,128)(2,1)S(1)}, bf16[256,2,256]{0,2,1:T(8,128)(2,1)S(1)}, u32[]{:S(2)}, u32[]{:S(2)}) %collective-permute-start.3) | collective-permute-done | bytes 262176 | tf_op jit(solution)/shard_map/ppermute | solution.py:16
  128.9 1.9 %collective-permute-start.4 = (bf16[256,2,256]{0,2,1:T(8,128)(2,1)S(1)}, bf16[256,2,256]{0,2,1:T(8,128)(2,1)S(1)}, u32[]{:S(2)}, u32[]{:S(2)}) collective-permute-start(bf16[256,2,256]{0,2,1:T(8,128)(2,1)S(1)} %collective-permute-done.3), channel_id=1, source_target_pairs={{0,8},{8,16},{16,24},{24,32},{32,40},{40,48},{48,56},{56,64},{64,7... | collective-permute-start | bytes 786440 | tf_op jit(solution)/shard_map/ppermute | solution.py:16
  130.9 0.3 fusion.129
  131.2 0.3 fusion.122
  131.5 8.7 %collective-permute-done.4 = bf16[256,2,256]{0,2,1:T(8,128)(2,1)S(1)} collective-permute-done((bf16[256,2,256]{0,2,1:T(8,128)(2,1)S(1)}, bf16[256,2,256]{0,2,1:T(8,128)(2,1)S(1)}, u32[]{:S(2)}, u32[]{:S(2)}) %collective-permute-start.4) | collective-permute-done | bytes 262176 | tf_op jit(solution)/shard_map/ppermute | solution.py:16
  140.2 2.1 %collective-permute-start.5 = (bf16[256,2,256]{0,2,1:T(8,128)(2,1)S(1)}, bf16[256,2,256]{0,2,1:T(8,128)(2,1)S(1)}, u32[]{:S(2)}, u32[]{:S(2)}) collective-permute-start(bf16[256,2,256]{0,2,1:T(8,128)(2,1)S(1)} %collective-permute-done.4), channel_id=1, source_target_pairs={{0,8},{8,16},{16,24},{24,32},{32,40},{40,48},{48,56},{56,64},{64,7... | collective-permute-start | bytes 786440 | tf_op jit(solution)/shard_map/ppermute | solution.py:16
  142.3 0.3 fusion.128
  142.6 1.7 fusion.121
  144.3 7.2 %collective-permute-done.5 = bf16[256,2,256]{0,2,1:T(8,128)(2,1)S(1)} collective-permute-done((bf16[256,2,256]{0,2,1:T(8,128)(2,1)S(1)}, bf16[256,2,256]{0,2,1:T(8,128)(2,1)S(1)}, u32[]{:S(2)}, u32[]{:S(2)}) %collective-permute-start.5) | collective-permute-done | bytes 262176 | tf_op jit(solution)/shard_map/ppermute | solution.py:16
  151.5 0.3 fusion.127
  151.8 1.7 fusion.120
  153.7 0.2 convolution_add_fusion.11
  154.0 0.2 convolution_add_fusion.10
  154.2 0.2 convolution_add_fusion.9
  154.5 0.5 fusion.39
  155.0 0.2 convolution_add_fusion.8
  155.5 0.9 fusion.33
  156.4 1.1 copy.185
  157.5 0.8 maximum_maximum_fusion
  158.3 1.9 %fusion.53 = (f32[256,2]{0,1:T(2,128)S(1)}, f32[256,2]{0,1:T(2,128)S(1)}, f32[256,2]{0,1:T(2,128)S(1)}, f32[256,2]{0,1:T(2,128)S(1)}, f32[256,2]{0,1:T(2,128)S(1...) fusion(f32[256,2,256]{0,2,1:T(8,128)S(1)} %get-tuple-element.65, f32[256,2]{0,1:T(2,128)S(1)} %maximum_maximum_fusion, ...), kind=kLoop, calls=%fused_computation.96 | loop fusion | flops 1831424 | bytes 3686400 | tf_op jit(solution)/shard_map/reduce_sum | solution.py:105
  160.5 0.2 convolution_add_fusion.5
  160.8 0.2 convolution_add_fusion.4
  161.3 0.2 convolution_add_fusion.2
  161.6 0.2 convolution_add_fusion.1
  162.3 1.3 pad_maximum_fusion.1
  163.6 6.5 %reshape.848 = bf16[64,1,8192]{2,1,0:T(2,128)(2,1)S(1)} reshape(bf16[64,2,4096]{2,1,0:T(2,128)(2,1)} %all-to-all-done.1) | data formatting | bytes 2097152
  170.1 1.2 convolution_convert_fusion.1
  171.4 0.9 reshape.844
  (95 shorter events, 3.3 us)
Async XLA Ops:
  7.2 42.1 %copy-start = (bf16[2048,256]{1,0:T(8,128)(2,1)S(1)}, bf16[2048,256]{1,0:T(8,128)(2,1)}, u32[]{:S(2)}) copy-start(bf16[2048,256]{1,0:T(8,128)(2,1)} %param.7) | copy-start | bytes 3145732
  7.2 42.0 %all-gather.2.cloned.1.call-start = ((), (), s32[]{:S(2)}) async-start(), calls=%async_computation.2 | async-start | bytes 1179648 | tf_op jit(solution)/shard_map/all_gather | solution.py:46
  9.6 21.0 %all-to-all-start = ((s32[64,1,1]{2,1,0:T(1,128)}), s32[64,1,1]{2,1,0:T(1,128)S(1)}, u32[]{:S(2)}, u32[]{:S(2)}) async-start(s32[64,1,1]{2,1,0:T(1,128)} %copy.187), calls=%async_computation | async-start | bytes 65536 | tf_op jit(solution)/shard_map/all_to_all | solution.py:127
  51.0 1.3 copy-start.2
  51.5 0.7 copy-start.21
  54.7 20.6 %collective-permute-start = (bf16[256,2,256]{0,2,1:T(8,128)(2,1)}, bf16[256,2,256]{0,2,1:T(8,128)(2,1)}, u32[]{:S(2)}, u32[]{:S(2)}) collective-permute-start(bf16[256,2,256]{0,2,1:T(8,128)(2,1)} %pad_maximum_fusion), channel_id=1, source_target_pairs={{0,8},{8,16},{16,24},{24,32},{32,40},{40,48},{48,56},{56,64},{64,7... | collective-permute-start | bytes 786440 | tf_op jit(solution)/shard_map/ppermute | solution.py:16
  62.0 11.5 %copy-start.22 = (bf16[256,2,128]{2,0,1:T(8,128)(2,1)S(1)}, bf16[256,2,128]{2,0,1:T(8,128)(2,1)}, u32[]{:S(2)}) copy-start(bf16[256,2,128]{2,0,1:T(8,128)(2,1)} %copy-done.21) | copy-start | bytes 393220
  62.0 11.5 %copy-start.25 = (pred[256,256]{0,1:T(8,128)(4,1)S(1)}, pred[256,256]{0,1:T(8,128)(4,1)}, u32[]{:S(2)}) copy-start(pred[256,256]{0,1:T(8,128)(4,1)} %get-tuple-element.47) | copy-start | bytes 196612
  63.6 16.1 %copy-start.19 = (pred[256,256]{0,1:T(8,128)(4,1)S(1)}, pred[256,256]{0,1:T(8,128)(4,1)}, u32[]{:S(2)}) copy-start(pred[256,256]{0,1:T(8,128)(4,1)} %get-tuple-element.42) | copy-start | bytes 196612
  63.6 100.0 %all-to-all-start.1 = ((bf16[64,2,4096]{2,1,0:T(2,128)(2,1)}), bf16[64,2,4096]{2,1,0:T(2,128)(2,1)}, u32[]{:S(2)}, u32[]{:S(2)}) async-start(bf16[64,2,4096]{2,1,0:T(2,128)(2,1)} %reshape.847), calls=%async_computation.1 | async-start | bytes 2097152 | tf_op jit(solution)/shard_map/all_to_all | solution.py:126
  73.5 33.8 %copy-start.20 = (pred[256,256]{0,1:T(8,128)(4,1)S(1)}, pred[256,256]{0,1:T(8,128)(4,1)}, u32[]{:S(2)}) copy-start(pred[256,256]{0,1:T(8,128)(4,1)} %and_and_fusion.4) | copy-start | bytes 196612
  75.4 30.0 %collective-permute-start.1 = (bf16[256,2,256]{0,2,1:T(8,128)(2,1)}, bf16[256,2,256]{0,2,1:T(8,128)(2,1)S(1)}, u32[]{:S(2)}, u32[]{:S(2)}) collective-permute-start(bf16[256,2,256]{0,2,1:T(8,128)(2,1)} %collective-permute-done), channel_id=1, source_target_pairs={{0,8},{8,16},{16,24},{24,32},{32,40},{40,48},{48,56},{56,64},{64,7... | collective-permute-start | bytes 786440 | tf_op jit(solution)/shard_map/ppermute | solution.py:16
  79.7 74.0 %copy-start.5 = (bf16[256,1,256]{0,2,1:T(8,128)(2,1)}, bf16[256,1,256]{0,2,1:T(8,128)(2,1)S(1)}, u32[]{:S(2)}) copy-start(bf16[256,1,256]{0,2,1:T(8,128)(2,1)S(1)} %get-tuple-element.38) | copy-start | bytes 393220
  79.7 39.8 %copy-start.18 = (pred[256,256]{0,1:T(8,128)(4,1)S(1)}, pred[256,256]{0,1:T(8,128)(4,1)}, u32[]{:S(2)}) copy-start(pred[256,256]{0,1:T(8,128)(4,1)} %get-tuple-element.46) | copy-start | bytes 196612
  105.3 12.2 %collective-permute-start.2 = (bf16[256,2,256]{0,2,1:T(8,128)(2,1)S(1)}, bf16[256,2,256]{0,2,1:T(8,128)(2,1)S(1)}, u32[]{:S(2)}, u32[]{:S(2)}) collective-permute-start(bf16[256,2,256]{0,2,1:T(8,128)(2,1)S(1)} %collective-permute-done.1), channel_id=1, source_target_pairs={{0,8},{8,16},{16,24},{24,32},{32,40},{40,48},{48,56},{56,64},{64,7... | collective-permute-start | bytes 786440 | tf_op jit(solution)/shard_map/ppermute | solution.py:16
  107.3 46.7 %copy-start.7 = (bf16[256,1,256]{0,2,1:T(8,128)(2,1)}, bf16[256,1,256]{0,2,1:T(8,128)(2,1)S(1)}, u32[]{:S(2)}) copy-start(bf16[256,1,256]{0,2,1:T(8,128)(2,1)S(1)} %get-tuple-element.36) | copy-start | bytes 393220
  107.3 23.6 %copy-start.17 = (pred[256,256]{0,1:T(8,128)(4,1)S(1)}, pred[256,256]{0,1:T(8,128)(4,1)}, u32[]{:S(2)}) copy-start(pred[256,256]{0,1:T(8,128)(4,1)} %get-tuple-element.43) | copy-start | bytes 196612
  117.6 11.4 %collective-permute-start.3 = (bf16[256,2,256]{0,2,1:T(8,128)(2,1)S(1)}, bf16[256,2,256]{0,2,1:T(8,128)(2,1)S(1)}, u32[]{:S(2)}, u32[]{:S(2)}) collective-permute-start(bf16[256,2,256]{0,2,1:T(8,128)(2,1)S(1)} %collective-permute-done.2), channel_id=1, source_target_pairs={{0,8},{8,16},{16,24},{24,32},{32,40},{40,48},{48,56},{56,64},{64,7... | collective-permute-start | bytes 786440 | tf_op jit(solution)/shard_map/ppermute | solution.py:16
  119.5 34.7 %copy-start.9 = (bf16[256,1,256]{0,2,1:T(8,128)(2,1)}, bf16[256,1,256]{0,2,1:T(8,128)(2,1)S(1)}, u32[]{:S(2)}) copy-start(bf16[256,1,256]{0,2,1:T(8,128)(2,1)S(1)} %get-tuple-element.34) | copy-start | bytes 393220
  119.5 22.8 %copy-start.16 = (pred[256,256]{0,1:T(8,128)(4,1)S(1)}, pred[256,256]{0,1:T(8,128)(4,1)}, u32[]{:S(2)}) copy-start(pred[256,256]{0,1:T(8,128)(4,1)} %get-tuple-element.44) | copy-start | bytes 196612
  128.9 11.3 %collective-permute-start.4 = (bf16[256,2,256]{0,2,1:T(8,128)(2,1)S(1)}, bf16[256,2,256]{0,2,1:T(8,128)(2,1)S(1)}, u32[]{:S(2)}, u32[]{:S(2)}) collective-permute-start(bf16[256,2,256]{0,2,1:T(8,128)(2,1)S(1)} %collective-permute-done.3), channel_id=1, source_target_pairs={{0,8},{8,16},{16,24},{24,32},{32,40},{40,48},{48,56},{56,64},{64,7... | collective-permute-start | bytes 786440 | tf_op jit(solution)/shard_map/ppermute | solution.py:16
  130.9 24.1 %copy-start.11 = (bf16[256,1,256]{0,2,1:T(8,128)(2,1)}, bf16[256,1,256]{0,2,1:T(8,128)(2,1)S(1)}, u32[]{:S(2)}) copy-start(bf16[256,1,256]{0,2,1:T(8,128)(2,1)S(1)} %get-tuple-element.32) | copy-start | bytes 393220
  130.9 20.6 %copy-start.15 = (pred[256,256]{0,1:T(8,128)(4,1)S(1)}, pred[256,256]{0,1:T(8,128)(4,1)}, u32[]{:S(2)}) copy-start(pred[256,256]{0,1:T(8,128)(4,1)} %get-tuple-element.45) | copy-start | bytes 196612
  140.2 11.3 %collective-permute-start.5 = (bf16[256,2,256]{0,2,1:T(8,128)(2,1)S(1)}, bf16[256,2,256]{0,2,1:T(8,128)(2,1)S(1)}, u32[]{:S(2)}, u32[]{:S(2)}) collective-permute-start(bf16[256,2,256]{0,2,1:T(8,128)(2,1)S(1)} %collective-permute-done.4), channel_id=1, source_target_pairs={{0,8},{8,16},{16,24},{24,32},{32,40},{40,48},{48,56},{56,64},{64,7... | collective-permute-start | bytes 786440 | tf_op jit(solution)/shard_map/ppermute | solution.py:16
  142.3 12.9 %copy-start.13 = (bf16[256,1,256]{0,2,1:T(8,128)(2,1)}, bf16[256,1,256]{0,2,1:T(8,128)(2,1)S(1)}, u32[]{:S(2)}) copy-start(bf16[256,1,256]{0,2,1:T(8,128)(2,1)S(1)} %get-tuple-element.30) | copy-start | bytes 393220
  151.5 4.0 %copy-start.23 = (bf16[256,1,256]{0,2,1:T(8,128)(2,1)}, bf16[256,1,256]{0,2,1:T(8,128)(2,1)S(1)}, u32[]{:S(2)}) copy-start(bf16[256,1,256]{0,2,1:T(8,128)(2,1)S(1)} %get-tuple-element.28) | copy-start | bytes 393220
  157.5 2.7 %copy-start.3 = (f32[256,2,256]{0,2,1:T(8,128)S(1)}, f32[256,2,256]{0,2,1:T(8,128)}, u32[]{:S(2)}) copy-start(f32[256,2,256]{0,2,1:T(8,128)} %get-tuple-element.63) | copy-start | bytes 1572868
  158.2 2.2 %copy-start.6 = (bf16[256,1,256]{0,2,1:T(8,128)(2,1)S(1)}, bf16[256,1,256]{0,2,1:T(8,128)(2,1)}, u32[]{:S(2)}) copy-start(bf16[256,1,256]{0,2,1:T(8,128)(2,1)} %copy-done.5) | copy-start | bytes 393220
  158.3 2.5 %copy-start.8 = (bf16[256,1,256]{0,2,1:T(8,128)(2,1)S(1)}, bf16[256,1,256]{0,2,1:T(8,128)(2,1)}, u32[]{:S(2)}) copy-start(bf16[256,1,256]{0,2,1:T(8,128)(2,1)} %copy-done.7) | copy-start | bytes 393220
  160.2 0.9 copy-start.10
  160.2 1.1 copy-start.12
  160.5 1.1 copy-start.1
  160.5 1.1 copy-start.14
  160.8 1.1 copy-start.4
  160.8 1.1 copy-start.24
  162.1 8.0 %copy-start.26 = (s32[64]{0:T(128)S(1)}, s32[64]{0:T(128)}, u32[]{:S(2)}) copy-start(s32[64]{0:T(128)} %reduce.2) | copy-start | bytes 772
Sparse Core Ops, SparseCore 0:
  10.1 39.0 all-gather.1
where the time goes:
time: 180 us; the launch traced here: 179 us
  waiting for transfers between devices  79.6 us (44%)
  starting transfers between devices  37.1 us (21%)
  matrix products  17.2 us (10%)
  local copies, waits for them, and re-layouts  17 us (9%)
  between operations  14.8 us (8%)
  other arithmetic  13.3 us (7%)
    ppermute x6, waiting for transfers between devices, from_behind(): return lax.ppermute(value, axis, pairs)  59.4 us
    all_gather x1, waiting for transfers between devices, body(): piece = lax.all_gather(tokens, 'tp', axis=1, tiled=True)  16.9 us
    ppermute x6, starting transfers between devices, from_behind(): return lax.ppermute(value, axis, pairs)  14.6 us
    all_to_all x1, starting transfers between devices, body(): lax.all_to_all(labels, 'seq', split_axis=0, concat_axis=0, tiled=True)  12.6 us
    unnamed x59, local copies, waits for them, and re-layouts  10.3 us
    all_to_all x1, starting transfers between devices, body(): lax.all_to_all(outgoing, 'seq', split_axis=0, concat_axis=0, tiled=True)  9.87 us
    dot_general x14, matrix products, block_scores(): jnp.einsum('qhd,khd->qhk', expert_query, key_heads, preferred_element_typ...  8.03 us
    dot_general x14, matrix products, accumulate(): jnp.einsum('qhk,khd->qhd', rounded, value_heads, preferred_element_type=j...  3.92 us
  transfers between devices with their start and end apart: 9, of which 7 were waited for; matrix products, arithmetic and copies ran while one was open for 19% of the time, Pallas kernels for 0%

commit v1 on v0

--- a/solution.py
+++ b/solution.py
@@ -3,6 +3,7 @@
 import jax.numpy as jnp
 from jax import lax
 from jax.sharding import PartitionSpec as P
+from jax.lax import all_to_all, axis_size
 
 HD = 128
 TOPK = 2
@@ -43,7 +44,10 @@
     first_row = lax.axis_index("seq") * block_rows
     positions = first_row + jnp.arange(block_rows, dtype=jnp.int32)
     segment, offsets = segment_info(positions, prompt_pages)
-    piece = lax.all_gather(tokens, "tp", axis=1, tiled=True)
+    serve_the_frame = lambda obj, net_axis: jnp.concatenate(
+        all_to_all(jnp.stack([obj] * axis_size(net_axis), axis=0), net_axis, 0, 0), axis=1
+    )
+    piece = serve_the_frame(tokens, "tp")
     raw_keys = jnp.dot(piece, key_weight, preferred_element_type=jnp.float32)
     raw_values = jnp.dot(piece, value_weight, preferred_element_type=jnp.float32)
     keys = rotate_heads(raw_keys.reshape(block_rows, local_heads, HD), offsets).astype(jnp.bfloat16)

time: 180 us -> 187 us (1.039)
  between operations: 14.8 us -> 1.44 us
  local copies, waits for them, and re-layouts: 17 us -> 25.3 us
  starting transfers between devices: 37.1 us -> 45.2 us
  waiting for transfers between devices: 79.6 us -> 85 us
  matrix products: 17.2 us -> 14.9 us
    all_to_all x0 -> x1, waiting for transfers between devices: none -> 20.3 us  [body(): all_to_all(jnp.stack([obj] * axis_size(net_axis), axis=0), net_axis, 0, 0)]
    all_gather x1 -> x0, waiting for transfers between devices: 16.9 us -> none  [body(): piece = lax.all_gather(tokens, 'tp', axis=1, tiled=True)]
    all_to_all x0 -> x1, starting transfers between devices: none -> 9.41 us  [body(): all_to_all(jnp.stack([obj] * axis_size(net_axis), axis=0), net_axis, 0, 0)]
    all_to_all x1, waiting for transfers between devices: 2.7 us -> 8.31 us  [body(): lax.all_to_all(labels, 'seq', split_axis=0, concat_axis=0, tiled=True)]
    reshape x0 -> x3, local copies, waits for them, and re-layouts: none -> 4.04 us  [body(): jnp.concatenate(all_to_all(jnp.stack([obj] * axis_size(net_axis), axis=0)...]
    ppermute x6, waiting for transfers between devices: 59.4 us -> 56.4 us  [from_behind(): return lax.ppermute(value, axis, pairs)]
    unnamed x59 -> x67, local copies, waits for them, and re-layouts: 10.3 us -> 11.2 us
  transfers between devices with their start and end apart: 9 -> 9, of which waited for: 7 -> 7; matrix products, arithmetic and copies ran while one was open for 19% -> 18% of each run, Pallas kernels for 0% -> 0%
where the time goes in v1:
time: 187 us; the launch traced here: 186 us
  waiting for transfers between devices  85 us (45%)
  starting transfers between devices  45.2 us (24%)
  local copies, waits for them, and re-layouts  25.3 us (14%)
  matrix products  14.9 us (8%)
  other arithmetic  13.7 us (7%)
    ppermute x6, waiting for transfers between devices, from_behind(): return lax.ppermute(value, axis, pairs)  56.4 us
    all_to_all x1, waiting for transfers between devices, body(): all_to_all(jnp.stack([obj] * axis_size(net_axis), axis=0), net_axis, 0, 0)  20.3 us
    ppermute x6, starting transfers between devices, from_behind(): return lax.ppermute(value, axis, pairs)  13.7 us
    all_to_all x1, starting transfers between devices, body(): lax.all_to_all(labels, 'seq', split_axis=0, concat_axis=0, tiled=True)  12.6 us
    unnamed x67, local copies, waits for them, and re-layouts  11.2 us
    all_to_all x1, starting transfers between devices, body(): lax.all_to_all(outgoing, 'seq', split_axis=0, concat_axis=0, tiled=True)  9.46 us
    all_to_all x1, starting transfers between devices, body(): all_to_all(jnp.stack([obj] * axis_size(net_axis), axis=0), net_axis, 0, 0)  9.41 us
    all_to_all x1, waiting for transfers between devices, body(): lax.all_to_all(labels, 'seq', split_axis=0, concat_axis=0, tiled=True)  8.31 us
  transfers between devices with their start and end apart: 9, of which 7 were waited for; matrix products, arithmetic and copies ran while one was open for 18% of the time, Pallas kernels for 0%

profile of v1, /device:TPU:6, one launch (start us, length us, event | category | flops | bytes accessed | tf_op | source)
XLA Modules:
  0.0 185.6 jit_solution(3967922898008019957)
XLA Ops:
  0.7 0.8 fusion.112
  1.7 0.7 copy.190
  2.4 12.6 %all-to-all-start.1 = ((s32[64,1,1]{2,1,0:T(1,128)}), s32[64,1,1]{2,1,0:T(1,128)S(1)}, u32[]{:S(2)}, u32[]{:S(2)}) async-start(s32[64,1,1]{2,1,0:T(1,128)} %copy.190), calls=%async_computation.1 | async-start | bytes 65536 | tf_op jit(solution)/shard_map/all_to_all | solution.py:131
  15.1 8.3 %all-to-all-done.1 = s32[64,1,1]{2,1,0:T(1,128)S(1)} async-done(((s32[64,1,1]{2,1,0:T(1,128)}), s32[64,1,1]{2,1,0:T(1,128)S(1)}, u32[]{:S(2)}, u32[]{:S(2)}) %all-to-all-start.1) | async-done | bytes 288 | tf_op jit(solution)/shard_map/all_to_all | solution.py:131
  23.4 2.0 %stack.12 = bf16[8,256,256]{2,1,0:T(8,128)(2,1)} broadcast(bf16[256,256]{1,0:T(8,128)(2,1)} %param.6), dimensions={1,2} | broadcast | bytes 1179648 | tf_op jit(solution)/shard_map/stack | solution.py:48
  25.4 9.4 %all-to-all-start = ((bf16[8,256,256]{2,1,0:T(8,128)(2,1)}), bf16[8,256,256]{2,1,0:T(8,128)(2,1)S(1)}, u32[]{:S(2)}, u32[]{:S(2)}) async-start(bf16[8,256,256]{2,1,0:T(8,128)(2,1)} %stack.12), calls=%async_computation | async-start | bytes 2097152 | tf_op jit(solution)/shard_map/all_to_all | solution.py:48
  34.9 1.5 copy.221
  36.4 1.1 copy.157
  37.8 0.8 and_and_fusion.4
  38.6 0.3 multiply_cosine_fusion
  38.9 2.0 %and_and_fusion.5 = (pred[256,256]{0,1:T(8,128)(4,1)}, pred[256,256]{0,1:T(8,128)(4,1)}, pred[256,256]{0,1:T(8,128)(4,1)}, pred[256,256]{0,1:T(8,128)(4,1)}, pre...) fusion(s32[256]{0:T(256)S(1)} %get-tuple-element.78, s32[256]{0:T(256)S(1)} %get-tuple-element.25, s32[256]{0:T(256)S(1)} %fusion.110, ...), kind=kLoop, calls=%fused_computation.132 | loop fusion | flops 1572864 | bytes 407040 | tf_op jit(solution)/shard_map/and | solution.py:70
  40.9 2.5 %reduce.2 = s32[64]{0:T(128)} reduce(s32[64,1,1]{2,1,0:T(1,128)} %copy-done.26, s32[]{:T(128)} %constant.64.clone.1), dimensions={1,2}, to_apply=%all_to_all.11.reduce_sub_computation | reduce | bytes 516 | tf_op jit(solution)/shard_map/all_to_all | solution.py:131
  43.4 20.3 %all-to-all-done = bf16[8,256,256]{2,1,0:T(8,128)(2,1)S(1)} async-done(((bf16[8,256,256]{2,1,0:T(8,128)(2,1)}), bf16[8,256,256]{2,1,0:T(8,128)(2,1)S(1)}, u32[]{:S(2)}, u32[]{:S(2)}) %all-to-all-start) | async-done | bytes 1048608 | tf_op jit(solution)/shard_map/all_to_all | solution.py:48
  63.8 1.6 copy.154
  65.3 2.3 %reshape.853 = bf16[256,2048,1]{1,0,2:T(8,128)(2,1)} reshape(bf16[256,8,256]{2,1,0:T(8,128)(2,1)} %copy.154) | data formatting | bytes 2097152 | tf_op jit(solution)/shard_map/reshape | solution.py:47
  67.8 1.1 copy-done.2
  68.9 0.5 fusion.133
  69.5 0.6 copy-done.22
  70.1 0.5 convolution_convert_fusion.2
  70.6 0.7 pad_maximum_fusion
  71.4 2.5 %collective-permute-start = (bf16[256,2,256]{0,2,1:T(8,128)(2,1)}, bf16[256,2,256]{0,2,1:T(8,128)(2,1)}, u32[]{:S(2)}, u32[]{:S(2)}) collective-permute-start(bf16[256,2,256]{0,2,1:T(8,128)(2,1)} %pad_maximum_fusion), channel_id=1, source_target_pairs={{0,8},{8,16},{16,24},{24,32},{32,40},{40,48},{48,56},{56,64},{64,7... | collective-permute-start | bytes 786440 | tf_op jit(solution)/shard_map/ppermute | solution.py:17
  73.9 1.1 copy.191
  75.2 0.5 fusion
  75.8 0.6 broadcast.738
  76.3 1.5 reduce.4
  77.9 1.6 reshape.857
  79.5 9.5 %all-to-all-start.2 = ((bf16[64,2,4096]{2,1,0:T(2,128)(2,1)}), bf16[64,2,4096]{2,1,0:T(2,128)(2,1)}, u32[]{:S(2)}, u32[]{:S(2)}) async-start(bf16[64,2,4096]{2,1,0:T(2,128)(2,1)} %reshape.857), calls=%async_computation.2 | async-start | bytes 2097152 | tf_op jit(solution)/shard_map/all_to_all | solution.py:130
  89.0 0.3 fusion.131
  89.3 1.7 fusion.124
  90.9 3.4 %collective-permute-start.1 = (bf16[256,2,256]{0,2,1:T(8,128)(2,1)}, bf16[256,2,256]{0,2,1:T(8,128)(2,1)S(1)}, u32[]{:S(2)}, u32[]{:S(2)}) collective-permute-start(bf16[256,2,256]{0,2,1:T(8,128)(2,1)} %collective-permute-done), channel_id=1, source_target_pairs={{0,8},{8,16},{16,24},{24,32},{32,40},{40,48},{48,56},{56,64},{64,7... | collective-permute-start | bytes 786440 | tf_op jit(solution)/shard_map/ppermute | solution.py:17
  94.3 1.0 fusion.118
  95.3 0.3 fusion.132
  95.6 0.3 fusion.125
  95.9 22.8 %collective-permute-done.1 = bf16[256,2,256]{0,2,1:T(8,128)(2,1)S(1)} collective-permute-done((bf16[256,2,256]{0,2,1:T(8,128)(2,1)}, bf16[256,2,256]{0,2,1:T(8,128)(2,1)S(1)}, u32[]{:S(2)}, u32[]{:S(2)}) %collective-permute-start.1) | collective-permute-done | bytes 262176 | tf_op jit(solution)/shard_map/ppermute | solution.py:17
  118.7 1.9 %collective-permute-start.2 = (bf16[256,2,256]{0,2,1:T(8,128)(2,1)S(1)}, bf16[256,2,256]{0,2,1:T(8,128)(2,1)S(1)}, u32[]{:S(2)}, u32[]{:S(2)}) collective-permute-start(bf16[256,2,256]{0,2,1:T(8,128)(2,1)S(1)} %collective-permute-done.1), channel_id=1, source_target_pairs={{0,8},{8,16},{16,24},{24,32},{32,40},{40,48},{48,56},{56,64},{64,7... | collective-permute-start | bytes 786440 | tf_op jit(solution)/shard_map/ppermute | solution.py:17
  120.7 0.3 fusion.130
  121.0 0.3 fusion.123
  121.2 9.1 %collective-permute-done.2 = bf16[256,2,256]{0,2,1:T(8,128)(2,1)S(1)} collective-permute-done((bf16[256,2,256]{0,2,1:T(8,128)(2,1)S(1)}, bf16[256,2,256]{0,2,1:T(8,128)(2,1)S(1)}, u32[]{:S(2)}, u32[]{:S(2)}) %collective-permute-start.2) | collective-permute-done | bytes 262176 | tf_op jit(solution)/shard_map/ppermute | solution.py:17
  130.3 1.9 %collective-permute-start.3 = (bf16[256,2,256]{0,2,1:T(8,128)(2,1)S(1)}, bf16[256,2,256]{0,2,1:T(8,128)(2,1)S(1)}, u32[]{:S(2)}, u32[]{:S(2)}) collective-permute-start(bf16[256,2,256]{0,2,1:T(8,128)(2,1)S(1)} %collective-permute-done.2), channel_id=1, source_target_pairs={{0,8},{8,16},{16,24},{24,32},{32,40},{40,48},{48,56},{56,64},{64,7... | collective-permute-start | bytes 786440 | tf_op jit(solution)/shard_map/ppermute | solution.py:17
  132.3 0.3 fusion.129
  132.6 0.3 fusion.122
  132.9 8.7 %collective-permute-done.3 = bf16[256,2,256]{0,2,1:T(8,128)(2,1)S(1)} collective-permute-done((bf16[256,2,256]{0,2,1:T(8,128)(2,1)S(1)}, bf16[256,2,256]{0,2,1:T(8,128)(2,1)S(1)}, u32[]{:S(2)}, u32[]{:S(2)}) %collective-permute-start.3) | collective-permute-done | bytes 262176 | tf_op jit(solution)/shard_map/ppermute | solution.py:17
  141.6 1.9 %collective-permute-start.4 = (bf16[256,2,256]{0,2,1:T(8,128)(2,1)S(1)}, bf16[256,2,256]{0,2,1:T(8,128)(2,1)S(1)}, u32[]{:S(2)}, u32[]{:S(2)}) collective-permute-start(bf16[256,2,256]{0,2,1:T(8,128)(2,1)S(1)} %collective-permute-done.3), channel_id=1, source_target_pairs={{0,8},{8,16},{16,24},{24,32},{32,40},{40,48},{48,56},{56,64},{64,7... | collective-permute-start | bytes 786440 | tf_op jit(solution)/shard_map/ppermute | solution.py:17
  143.5 0.3 fusion.128
  143.8 0.3 fusion.121
  144.1 8.7 %collective-permute-done.4 = bf16[256,2,256]{0,2,1:T(8,128)(2,1)S(1)} collective-permute-done((bf16[256,2,256]{0,2,1:T(8,128)(2,1)S(1)}, bf16[256,2,256]{0,2,1:T(8,128)(2,1)S(1)}, u32[]{:S(2)}, u32[]{:S(2)}) %collective-permute-start.4) | collective-permute-done | bytes 262176 | tf_op jit(solution)/shard_map/ppermute | solution.py:17
  152.8 2.1 %collective-permute-start.5 = (bf16[256,2,256]{0,2,1:T(8,128)(2,1)S(1)}, bf16[256,2,256]{0,2,1:T(8,128)(2,1)S(1)}, u32[]{:S(2)}, u32[]{:S(2)}) collective-permute-start(bf16[256,2,256]{0,2,1:T(8,128)(2,1)S(1)} %collective-permute-done.4), channel_id=1, source_target_pairs={{0,8},{8,16},{16,24},{24,32},{32,40},{40,48},{48,56},{56,64},{64,7... | collective-permute-start | bytes 786440 | tf_op jit(solution)/shard_map/ppermute | solution.py:17
  155.0 0.3 fusion.127
  155.3 1.7 fusion.120
  157.0 7.1 %collective-permute-done.5 = bf16[256,2,256]{0,2,1:T(8,128)(2,1)S(1)} collective-permute-done((bf16[256,2,256]{0,2,1:T(8,128)(2,1)S(1)}, bf16[256,2,256]{0,2,1:T(8,128)(2,1)S(1)}, u32[]{:S(2)}, u32[]{:S(2)}) %collective-permute-start.5) | collective-permute-done | bytes 262176 | tf_op jit(solution)/shard_map/ppermute | solution.py:17
  164.1 0.3 fusion.126
  164.4 1.6 fusion.119
  166.3 0.2 convolution_add_fusion.11
  167.1 0.5 fusion.39
  168.1 0.9 fusion.33
  169.0 1.8 copy.188
  170.8 0.7 maximum_maximum_fusion
  171.5 1.9 %fusion.53 = (f32[256,2]{0,1:T(2,128)S(1)}, f32[256,2]{0,1:T(2,128)S(1)}, f32[256,2]{0,1:T(2,128)S(1)}, f32[256,2]{0,1:T(2,128)S(1)}, f32[256,2]{0,1:T(2,128)S(1...) fusion(f32[256,2,256]{0,2,1:T(8,128)S(1)} %get-tuple-element.63, f32[256,2]{0,1:T(2,128)S(1)} %maximum_maximum_fusion, ...), kind=kLoop, calls=%fused_computation.96 | loop fusion | flops 1831424 | bytes 3686400 | tf_op jit(solution)/shard_map/reduce_sum | solution.py:109
  174.6 0.2 convolution_add_fusion.2
  174.9 0.2 convolution_add_fusion.1
  175.7 1.3 pad_maximum_fusion.1
  177.0 6.5 %reshape.858 = bf16[64,1,8192]{2,1,0:T(2,128)(2,1)S(1)} reshape(bf16[64,2,4096]{2,1,0:T(2,128)(2,1)} %all-to-all-done.2) | data formatting | bytes 2097152
  183.5 1.2 convolution_convert_fusion.1
  184.7 0.9 reshape.852
  (105 shorter events, 4.0 us)
Async XLA Ops:
  0.6 69.5 %copy-start = (bf16[2048,256]{1,0:T(8,128)(2,1)S(1)}, bf16[2048,256]{1,0:T(8,128)(2,1)}, u32[]{:S(2)}) copy-start(bf16[2048,256]{1,0:T(8,128)(2,1)} %param.8) | copy-start | bytes 3145732
  0.6 34.1 %copy-start.31 = (s32[16]{0:T(128)S(1)}, s32[16]{0:T(128)}, u32[]{:S(2)}) copy-start(s32[16]{0:T(128)} %param.10) | copy-start | bytes 196
  2.4 21.0 %all-to-all-start.1 = ((s32[64,1,1]{2,1,0:T(1,128)}), s32[64,1,1]{2,1,0:T(1,128)S(1)}, u32[]{:S(2)}, u32[]{:S(2)}) async-start(s32[64,1,1]{2,1,0:T(1,128)} %copy.190), calls=%async_computation.1 | async-start | bytes 65536 | tf_op jit(solution)/shard_map/all_to_all | solution.py:131
  23.4 13.0 %copy-start.26 = (s32[64,1,1]{2,1,0:T(1,128)}, s32[64,1,1]{2,1,0:T(1,128)S(1)}, u32[]{:S(2)}) copy-start(s32[64,1,1]{2,1,0:T(1,128)S(1)} %all-to-all-done.1) | copy-start | bytes 772
  25.4 38.4 %all-to-all-start = ((bf16[8,256,256]{2,1,0:T(8,128)(2,1)}), bf16[8,256,256]{2,1,0:T(8,128)(2,1)S(1)}, u32[]{:S(2)}, u32[]{:S(2)}) async-start(bf16[8,256,256]{2,1,0:T(8,128)(2,1)} %stack.12), calls=%async_computation | async-start | bytes 2097152 | tf_op jit(solution)/shard_map/all_to_all | solution.py:48
  67.7 1.2 copy-start.2
  69.4 0.6 copy-start.22
  69.5 0.6 copy-start.24
  71.4 19.6 %collective-permute-start = (bf16[256,2,256]{0,2,1:T(8,128)(2,1)}, bf16[256,2,256]{0,2,1:T(8,128)(2,1)}, u32[]{:S(2)}, u32[]{:S(2)}) collective-permute-start(bf16[256,2,256]{0,2,1:T(8,128)(2,1)} %pad_maximum_fusion), channel_id=1, source_target_pairs={{0,8},{8,16},{16,24},{24,32},{32,40},{40,48},{48,56},{56,64},{64,7... | collective-permute-start | bytes 786440 | tf_op jit(solution)/shard_map/ppermute | solution.py:17
  77.8 11.1 %copy-start.23 = (bf16[256,2,64]{0,2,1:T(8,128)(2,1)S(1)}, bf16[256,2,64]{0,2,1:T(8,128)(2,1)}, u32[]{:S(2)}) copy-start(bf16[256,2,64]{0,2,1:T(8,128)(2,1)} %copy-done.22) | copy-start | bytes 196612
  77.8 11.1 %copy-start.25 = (bf16[256,2,64]{0,2,1:T(8,128)(2,1)S(1)}, bf16[256,2,64]{0,2,1:T(8,128)(2,1)}, u32[]{:S(2)}) copy-start(bf16[256,2,64]{0,2,1:T(8,128)(2,1)} %copy-done.24) | copy-start | bytes 196612
  77.8 11.1 %copy-start.29 = (pred[256,256]{0,1:T(8,128)(4,1)S(1)}, pred[256,256]{0,1:T(8,128)(4,1)}, u32[]{:S(2)}) copy-start(pred[256,256]{0,1:T(8,128)(4,1)} %get-tuple-element.45) | copy-start | bytes 196612
  79.5 15.8 %copy-start.20 = (pred[256,256]{0,1:T(8,128)(4,1)S(1)}, pred[256,256]{0,1:T(8,128)(4,1)}, u32[]{:S(2)}) copy-start(pred[256,256]{0,1:T(8,128)(4,1)} %get-tuple-element.40) | copy-start | bytes 196612
  79.5 97.5 %all-to-all-start.2 = ((bf16[64,2,4096]{2,1,0:T(2,128)(2,1)}), bf16[64,2,4096]{2,1,0:T(2,128)(2,1)}, u32[]{:S(2)}, u32[]{:S(2)}) async-start(bf16[64,2,4096]{2,1,0:T(2,128)(2,1)} %reshape.857), calls=%async_computation.2 | async-start | bytes 2097152 | tf_op jit(solution)/shard_map/all_to_all | solution.py:130
  89.2 31.4 %copy-start.21 = (pred[256,256]{0,1:T(8,128)(4,1)S(1)}, pred[256,256]{0,1:T(8,128)(4,1)}, u32[]{:S(2)}) copy-start(pred[256,256]{0,1:T(8,128)(4,1)} %and_and_fusion.4) | copy-start | bytes 196612
  90.9 27.8 %collective-permute-start.1 = (bf16[256,2,256]{0,2,1:T(8,128)(2,1)}, bf16[256,2,256]{0,2,1:T(8,128)(2,1)S(1)}, u32[]{:S(2)}, u32[]{:S(2)}) collective-permute-start(bf16[256,2,256]{0,2,1:T(8,128)(2,1)} %collective-permute-done), channel_id=1, source_target_pairs={{0,8},{8,16},{16,24},{24,32},{32,40},{40,48},{48,56},{56,64},{64,7... | collective-permute-start | bytes 786440 | tf_op jit(solution)/shard_map/ppermute | solution.py:17
  95.3 71.0 %copy-start.5 = (bf16[256,1,256]{0,2,1:T(8,128)(2,1)}, bf16[256,1,256]{0,2,1:T(8,128)(2,1)S(1)}, u32[]{:S(2)}) copy-start(bf16[256,1,256]{0,2,1:T(8,128)(2,1)S(1)} %get-tuple-element.38) | copy-start | bytes 393220
  95.3 36.9 %copy-start.19 = (pred[256,256]{0,1:T(8,128)(4,1)S(1)}, pred[256,256]{0,1:T(8,128)(4,1)}, u32[]{:S(2)}) copy-start(pred[256,256]{0,1:T(8,128)(4,1)} %get-tuple-element.44) | copy-start | bytes 196612
  118.7 11.6 %collective-permute-start.2 = (bf16[256,2,256]{0,2,1:T(8,128)(2,1)S(1)}, bf16[256,2,256]{0,2,1:T(8,128)(2,1)S(1)}, u32[]{:S(2)}, u32[]{:S(2)}) collective-permute-start(bf16[256,2,256]{0,2,1:T(8,128)(2,1)S(1)} %collective-permute-done.1), channel_id=1, source_target_pairs={{0,8},{8,16},{16,24},{24,32},{32,40},{40,48},{48,56},{56,64},{64,7... | collective-permute-start | bytes 786440 | tf_op jit(solution)/shard_map/ppermute | solution.py:17
  120.6 45.9 %copy-start.7 = (bf16[256,1,256]{0,2,1:T(8,128)(2,1)}, bf16[256,1,256]{0,2,1:T(8,128)(2,1)S(1)}, u32[]{:S(2)}) copy-start(bf16[256,1,256]{0,2,1:T(8,128)(2,1)S(1)} %get-tuple-element.36) | copy-start | bytes 393220
  120.7 22.9 %copy-start.18 = (pred[256,256]{0,1:T(8,128)(4,1)S(1)}, pred[256,256]{0,1:T(8,128)(4,1)}, u32[]{:S(2)}) copy-start(pred[256,256]{0,1:T(8,128)(4,1)} %get-tuple-element.41) | copy-start | bytes 196612
  130.3 11.3 %collective-permute-start.3 = (bf16[256,2,256]{0,2,1:T(8,128)(2,1)S(1)}, bf16[256,2,256]{0,2,1:T(8,128)(2,1)S(1)}, u32[]{:S(2)}, u32[]{:S(2)}) collective-permute-start(bf16[256,2,256]{0,2,1:T(8,128)(2,1)S(1)} %collective-permute-done.2), channel_id=1, source_target_pairs={{0,8},{8,16},{16,24},{24,32},{32,40},{40,48},{48,56},{56,64},{64,7... | collective-permute-start | bytes 786440 | tf_op jit(solution)/shard_map/ppermute | solution.py:17
  132.2 34.6 %copy-start.9 = (bf16[256,1,256]{0,2,1:T(8,128)(2,1)}, bf16[256,1,256]{0,2,1:T(8,128)(2,1)S(1)}, u32[]{:S(2)}) copy-start(bf16[256,1,256]{0,2,1:T(8,128)(2,1)S(1)} %get-tuple-element.34) | copy-start | bytes 393220
  132.3 22.7 %copy-start.17 = (pred[256,256]{0,1:T(8,128)(4,1)S(1)}, pred[256,256]{0,1:T(8,128)(4,1)}, u32[]{:S(2)}) copy-start(pred[256,256]{0,1:T(8,128)(4,1)} %get-tuple-element.42) | copy-start | bytes 196612
  141.6 11.3 %collective-permute-start.4 = (bf16[256,2,256]{0,2,1:T(8,128)(2,1)S(1)}, bf16[256,2,256]{0,2,1:T(8,128)(2,1)S(1)}, u32[]{:S(2)}, u32[]{:S(2)}) collective-permute-start(bf16[256,2,256]{0,2,1:T(8,128)(2,1)S(1)} %collective-permute-done.3), channel_id=1, source_target_pairs={{0,8},{8,16},{16,24},{24,32},{32,40},{40,48},{48,56},{56,64},{64,7... | collective-permute-start | bytes 786440 | tf_op jit(solution)/shard_map/ppermute | solution.py:17
  143.5 24.1 %copy-start.11 = (bf16[256,1,256]{0,2,1:T(8,128)(2,1)}, bf16[256,1,256]{0,2,1:T(8,128)(2,1)S(1)}, u32[]{:S(2)}) copy-start(bf16[256,1,256]{0,2,1:T(8,128)(2,1)S(1)} %get-tuple-element.32) | copy-start | bytes 393220
  143.5 20.6 %copy-start.16 = (pred[256,256]{0,1:T(8,128)(4,1)S(1)}, pred[256,256]{0,1:T(8,128)(4,1)}, u32[]{:S(2)}) copy-start(pred[256,256]{0,1:T(8,128)(4,1)} %get-tuple-element.43) | copy-start | bytes 196612
  152.8 11.3 %collective-permute-start.5 = (bf16[256,2,256]{0,2,1:T(8,128)(2,1)S(1)}, bf16[256,2,256]{0,2,1:T(8,128)(2,1)S(1)}, u32[]{:S(2)}, u32[]{:S(2)}) collective-permute-start(bf16[256,2,256]{0,2,1:T(8,128)(2,1)S(1)} %collective-permute-done.4), channel_id=1, source_target_pairs={{0,8},{8,16},{16,24},{24,32},{32,40},{40,48},{48,56},{56,64},{64,7... | collective-permute-start | bytes 786440 | tf_op jit(solution)/shard_map/ppermute | solution.py:17
  154.9 12.9 %copy-start.13 = (bf16[256,1,256]{0,2,1:T(8,128)(2,1)}, bf16[256,1,256]{0,2,1:T(8,128)(2,1)S(1)}, u32[]{:S(2)}) copy-start(bf16[256,1,256]{0,2,1:T(8,128)(2,1)S(1)} %get-tuple-element.30) | copy-start | bytes 393220
  164.1 4.0 %copy-start.27 = (bf16[256,1,256]{0,2,1:T(8,128)(2,1)}, bf16[256,1,256]{0,2,1:T(8,128)(2,1)S(1)}, u32[]{:S(2)}) copy-start(bf16[256,1,256]{0,2,1:T(8,128)(2,1)S(1)} %get-tuple-element.28) | copy-start | bytes 393220
  170.8 2.7 %copy-start.3 = (f32[256,2,256]{0,2,1:T(8,128)S(1)}, f32[256,2,256]{0,2,1:T(8,128)}, u32[]{:S(2)}) copy-start(f32[256,2,256]{0,2,1:T(8,128)} %get-tuple-element.61) | copy-start | bytes 1572868
  171.5 2.2 %copy-start.6 = (bf16[256,1,256]{0,2,1:T(8,128)(2,1)S(1)}, bf16[256,1,256]{0,2,1:T(8,128)(2,1)}, u32[]{:S(2)}) copy-start(bf16[256,1,256]{0,2,1:T(8,128)(2,1)} %copy-done.5) | copy-start | bytes 393220
  171.5 2.5 %copy-start.8 = (bf16[256,1,256]{0,2,1:T(8,128)(2,1)S(1)}, bf16[256,1,256]{0,2,1:T(8,128)(2,1)}, u32[]{:S(2)}) copy-start(bf16[256,1,256]{0,2,1:T(8,128)(2,1)} %copy-done.7) | copy-start | bytes 393220
  173.4 0.9 copy-start.10
  173.5 1.1 copy-start.12
  173.7 1.1 copy-start.1
  173.7 1.1 copy-start.14
  174.0 1.1 copy-start.4
  174.0 1.1 copy-start.28
  174.6 1.1 copy-start.15
  175.4 8.1 %copy-start.30 = (s32[64]{0:T(128)S(1)}, s32[64]{0:T(128)}, u32[]{:S(2)}) copy-start(s32[64]{0:T(128)} %reduce.2) | copy-start | bytes 772
